TPU v7x, 32 devices: a whole 2x2x4 slice. The times are simulated.
32 devices in a mesh: ctx: 16 (over z, y, core), head: 2 (over x).
Axes of the slice: x: 2, y: 2, z: 4, core: 2. Of those that a mesh axis runs over, the one named last changes fastest.
Arguments:
- queries: bfloat16 [2048, 1536], P('ctx', 'head'), may hold values from -45 to 45
- key_rows: bfloat16 [2048, 256], P('ctx', 'head'), may hold values from -5 to 5
- value_rows: bfloat16 [2048, 256], P('ctx', 'head'), may hold values from -18 to 18
- cotangent: bfloat16 [2048, 1536], P('ctx', 'head'), may hold values from -6 to 6
- trace_ids: int32 [2048], P('ctx'), may hold values from 0 to 15, never falling along the last dimension, each value on 1 to 512 neighbouring positions
- correct: int32 [16], replicated, may hold values from 0 to 16, as said below
- group_size: int32 [16], replicated, may hold values from 4 to 16
Outputs:
- log_totals: float32 [2048, 12], P('ctx', 'head')
- grad_queries: float32 [2048, 1536], P('ctx', 'head')
- grad_keys: bfloat16 [2048, 256], P('ctx', 'head')
- grad_values: bfloat16 [2048, 256], P('ctx', 'head')
Inputs may be any that keep to these rules, and one draw needn't show every extreme that they name: correct[g] is at most group_size[g].
All inputs are finite; a program needn't handle non-finite values.
Results may differ from a plain program's by a relative error of at most 0.0054.
Values may be sent and summed in bfloat16 or wider, within the bound.
No kernel may reach another device: no remote copies, remote signals or barrier semaphores. Data moves between devices by JAX's collectives and lax.ppermute only.
A program may use at most 64 MiB of HBM per device.

v0:
```python
import math
import jax
import jax.numpy as jnp
from jax import lax
from jax.sharding import PartitionSpec as P

PASSK = 4


def pass_rate(correct, group_size):
    counts = group_size.astype(jnp.float32)
    hit_counts = correct.astype(jnp.float32)
    product = jnp.ones_like(counts)
    for offset in range(PASSK):
        product = product * (counts - hit_counts - offset) / (counts - offset)
    return 1.0 - product


def body(queries, key_rows, value_rows, cotangent, trace_ids, correct, group_size):
    tok_rows = queries.shape[0]
    half_rows = tok_rows // 2
    row_width = queries.shape[1]
    head_dim = key_rows.shape[1]
    head_count = row_width // head_dim
    ctx_count = lax.axis_size("ctx")
    my_index = lax.axis_index("ctx")
    length = tok_rows * ctx_count
    score_scale = 1.0 / math.sqrt(head_dim)
    pass_rates = pass_rate(correct, group_size)
    traces = jnp.arange(pass_rates.shape[0], dtype=jnp.int32)
    weights = jnp.sum(
        jnp.where(trace_ids[:, None] == traces[None, :], pass_rates[None, :], 0.0), axis=1
    )
    out_grads = (weights[:, None] * cotangent.astype(jnp.float32)).astype(jnp.bfloat16)
    first_base = my_index * tok_rows
    second_base = first_base + half_rows
    local_pos = jnp.arange(half_rows, dtype=jnp.int32)
    positions = jnp.concatenate([first_base + local_pos, second_base + local_pos], 0)
    last_first = first_base + half_rows - 1
    last_second = second_base + half_rows - 1
    query_all = queries.reshape(tok_rows, head_count, head_dim)
    grad_all = out_grads.reshape(tok_rows, head_count, head_dim)

    def run_block(running, key_block, value_block, key_start, block_fn):
        need_first = (key_start <= last_first).astype(jnp.int32)
        need_second = (key_start <= last_second).astype(jnp.int32)
        branch_index = need_first + 2 * need_second

        def skip_block(values_in):
            return values_in

        def first_only(values_in):
            return block_fn((0, half_rows), values_in, key_block, value_block, key_start)

        def second_only(values_in):
            return block_fn((half_rows, tok_rows), values_in, key_block, value_block, key_start)

        def both_halves(values_in):
            return block_fn((0, tok_rows), values_in, key_block, value_block, key_start)

        return lax.switch(branch_index, [skip_block, first_only, second_only, both_halves], running)

    def forward_block(row_span, running, key_block, value_block, key_start):
        row_begin, row_end = row_span
        row_peak, row_total, weighted = running
        query_part = query_all[row_begin:row_end]
        grad_part = grad_all[row_begin:row_end]
        query_pos = positions[row_begin:row_end]
        scores = (
            jnp.einsum("tqd,kd->tqk", query_part, key_block, preferred_element_type=jnp.float32)
            * score_scale
        )
        key_pos = key_start + jnp.arange(key_block.shape[0], dtype=jnp.int32)
        visible = key_pos[None, None, :] <= query_pos[:, None, None]
        block_peak = jnp.max(jnp.where(visible, scores, -1e30), axis=2)
        old_peak = row_peak[row_begin:row_end]
        new_peak = jnp.maximum(old_peak, block_peak)
        exp_terms = jnp.where(visible, jnp.exp(scores - new_peak[:, :, None]), 0.0)
        grad_probs = jnp.einsum(
            "tqd,kd->tqk", grad_part, value_block, preferred_element_type=jnp.float32
        )
        shrink = jnp.exp(old_peak - new_peak)
        new_total = row_total[row_begin:row_end] * shrink + jnp.sum(exp_terms, axis=2)
        new_weighted = weighted[row_begin:row_end] * shrink + jnp.sum(
            exp_terms * grad_probs, axis=2
        )
        return (
            row_peak.at[row_begin:row_end].set(new_peak),
            row_total.at[row_begin:row_end].set(new_total),
            weighted.at[row_begin:row_end].set(new_weighted),
        )

    row_peak = jnp.full((tok_rows, head_count), -1e30, jnp.float32)
    row_total = jnp.zeros((tok_rows, head_count), jnp.float32)
    weighted = jnp.zeros((tok_rows, head_count), jnp.float32)
    key_piece = lax.all_gather(key_rows, "ctx", axis=0, tiled=True)
    value_piece = lax.all_gather(value_rows, "ctx", axis=0, tiled=True)
    piece_rows = key_piece.shape[0]
    block_rows = math.gcd(piece_rows, 512)

    def forward_step(step_index, statistics):
        offset = step_index * block_rows
        key_block = lax.dynamic_slice_in_dim(key_piece, offset, block_rows, 0)
        value_block = lax.dynamic_slice_in_dim(value_piece, offset, block_rows, 0)
        return run_block(statistics, key_block, value_block, offset, forward_block)

    statistics = lax.fori_loop(
        0, piece_rows // block_rows, forward_step, (row_peak, row_total, weighted)
    )
    folded = statistics + (key_piece, value_piece)
    row_peak, row_total, weighted, key_store, value_store = folded
    log_totals = row_peak + jnp.log(row_total)
    delta_rows = weighted / row_total

    def backward_block(row_span, running, key_block, value_block, key_start):
        row_begin, row_end = row_span
        grad_query, zero_block = running
        query_part = query_all[row_begin:row_end]
        grad_part = grad_all[row_begin:row_end]
        query_pos = positions[row_begin:row_end]
        scores = (
            jnp.einsum("tqd,kd->tqk", query_part, key_block, preferred_element_type=jnp.float32)
            * score_scale
        )
        key_pos = key_start + jnp.arange(key_block.shape[0], dtype=jnp.int32)
        visible = key_pos[None, None, :] <= query_pos[:, None, None]
        probabilities = jnp.where(
            visible, jnp.exp(scores - log_totals[row_begin:row_end][:, :, None]), 0.0
        )
        prob_bf16 = probabilities.astype(jnp.bfloat16)
        grad_probs = jnp.einsum(
            "tqd,kd->tqk", grad_part, value_block, preferred_element_type=jnp.float32
        )
        grad_scores = (
            probabilities * (grad_probs - delta_rows[row_begin:row_end][:, :, None])
        ).astype(jnp.bfloat16)
        query_add = (
            jnp.einsum("tqk,kd->tqd", grad_scores, key_block, preferred_element_type=jnp.float32)
            * score_scale
        )
        key_add = (
            jnp.einsum("tqk,tqd->kd", grad_scores, query_part, preferred_element_type=jnp.float32)
            * score_scale
        )
        value_add = jnp.einsum(
            "tqk,tqd->kd", prob_bf16, grad_part, preferred_element_type=jnp.float32
        )
        return (
            grad_query.at[row_begin:row_end].add(query_add),
            jnp.concatenate([key_add, value_add], 1),
        )

    query_zero = jnp.zeros((tok_rows, head_count, head_dim), jnp.float32)
    key_block_rows = math.gcd(length, 512)

    def backward_step(step_index, running):
        grad_query, partial_sums = running
        key_start = step_index * key_block_rows
        key_block = lax.dynamic_slice_in_dim(key_store, key_start, key_block_rows, 0)
        value_block = lax.dynamic_slice_in_dim(value_store, key_start, key_block_rows, 0)
        zero_block = jnp.zeros((key_block_rows, 2 * head_dim), jnp.float32)
        grad_query, block_sums = run_block(
            (grad_query, zero_block), key_block, value_block, key_start, backward_block
        )
        partial_sums = lax.dynamic_update_slice_in_dim(partial_sums, block_sums, key_start, 0)
        return (grad_query, partial_sums)

    grad_query, partial_sums = lax.fori_loop(
        0,
        length // key_block_rows,
        backward_step,
        (query_zero, jnp.zeros((length, 2 * head_dim), jnp.float32)),
    )
    reduced = jnp.sum(
        lax.all_to_all(
            partial_sums.reshape(ctx_count, tok_rows, 2 * head_dim),
            "ctx",
            split_axis=0,
            concat_axis=0,
            tiled=True,
        ),
        axis=0,
    )
    grad_keys = reduced[:, :head_dim].astype(jnp.bfloat16)
    grad_values = reduced[:, head_dim:].astype(jnp.bfloat16)
    query_grads = grad_query.reshape(tok_rows, row_width)
    return (log_totals, query_grads, grad_keys, grad_values)


def solution(mesh):
    return jax.shard_map(
        body,
        mesh=mesh,
        in_specs=(
            P("ctx", "head"),
            P("ctx", "head"),
            P("ctx", "head"),
            P("ctx", "head"),
            P("ctx"),
            P(),
            P(),
        ),
        out_specs=(P("ctx", "head"), P("ctx", "head"), P("ctx", "head"), P("ctx", "head")),
        check_vma=False,
    )
```

profile of v0, /device:TPU:13, one launch (start us, length us, event | category | flops | bytes accessed | tf_op | source)
XLA Modules:
  0.0 124.0 jit_solution(4631487437105801853)
XLA Ops:
  0.7 0.7 fusion.61
  1.4 0.7 select_reduce_fusion.3
  2.1 1.0 multiply_convert_fusion.1
  3.5 1.1 copy.72
  4.8 17.1 %all_gather.6 = bf16[2048,128]{1,0:T(8,128)(2,1)S(1)} all-gather(bf16[128,128]{1,0:T(8,128)(2,1)S(1)} %copy-done.1), channel_id=1, replica_groups=mesh['ctx'=16,'head'=2] {'ctx'}, dimensions={0}, use_global_device_ids=true | all-gather | bytes 557056 | tf_op jit(solution)/shard_map/all_gather | solution.py:96
  21.9 22.8 %all_gather.7 = bf16[2048,128]{1,0:T(8,128)(2,1)S(1)} all-gather(bf16[128,128]{1,0:T(8,128)(2,1)S(1)} %copy-done.2), channel_id=1, replica_groups=mesh['ctx'=16,'head'=2] {'ctx'}, dimensions={0}, use_global_device_ids=true | all-gather | bytes 557056 | tf_op jit(solution)/shard_map/all_gather | solution.py:97
  44.8 3.9 %while.53 = (s32[]{:T(128)}, f32[128,6]{0,1:T(8,128)S(1)}, f32[128,6]{0,1:T(8,128)S(1)}, f32[128,6]{0,1:T(8,128)S(1)}, s32[]{:T(128)}, /*index=5*/s32[]{:T(128)}...) while((s32[]{:T(128)}, f32[128,6]{0,1:T(8,128)S(1)}, ...), condition=%wide.region_15.0_spmd.clone, body=%wide.region_1.15_spmd.clone.sunk | while | flops 205327120 | bytes 6221379 | solution.py:107
  44.8 1.7 %conditional.6 = ((f32[128,6]{0,1:T(8,128)S(1)}, f32[128,6]{0,1:T(8,128)S(1)}, f32[128,6]{0,1:T(8,128)S(1)})) conditional(s32[]{:T(128)} %clamp.18, (f32[128,6]{0,1:T(8,128)S(1)}, f32[128,6]{0,1:T(8,128)S(1)}, f32[128,6]{0,1:T(8,128)S(1)}) %tuple.202, (f32[128,6]{0,1:T(8,128)S(1)}, s32[]{:T(128)}, s32[]{:T(128)}, ...), branch_computations={%region_2.2_spmd, %region_3.6_spmd, %region_7.10_spmd, %region_11.... | conditional | flops 205327104 | bytes 5696036 | solution.py:61
  45.0 0.5 select_reduce_fusion.2
  45.4 0.6 multiply_reduce_fusion
  46.0 0.5 fusion.20
  46.6 1.7 %conditional.6 = ((f32[128,6]{0,1:T(8,128)S(1)}, f32[128,6]{0,1:T(8,128)S(1)}, f32[128,6]{0,1:T(8,128)S(1)})) conditional(s32[]{:T(128)} %clamp.18, (f32[128,6]{0,1:T(8,128)S(1)}, f32[128,6]{0,1:T(8,128)S(1)}, f32[128,6]{0,1:T(8,128)S(1)}) %tuple.202, (f32[128,6]{0,1:T(8,128)S(1)}, s32[]{:T(128)}, s32[]{:T(128)}, ...), branch_computations={%region_2.2_spmd, %region_3.6_spmd, %region_7.10_spmd, %region_11.... | conditional | flops 205327104 | bytes 5696036 | solution.py:61
  46.8 0.5 select_reduce_fusion.2
  47.3 0.6 multiply_reduce_fusion
  47.8 0.5 fusion.20
  48.7 1.5 %broadcast_in_dim.124.clone = f32[2048,256]{1,0:T(8,128)} broadcast(f32[]{:T(128)} %constant.488.clone.1), dimensions={} | broadcast | bytes 2097156 | tf_op jit(solution)/shard_map/broadcast_in_dim | solution.py:172
  50.2 8.7 %while.54 = (s32[]{:T(128)}, f32[128,6,128]{2,0,1:T(8,128)S(1)}, f32[2048,256]{1,0:T(8,128)}, s32[]{:T(128)}, s32[]{:T(128)}, /*index=5*/bf16[2048,128]{1,0:T(8,...) while((s32[]{:T(128)}, f32[128,6,128]{2,0,1:T(8,128)S(1)}, ...), condition=%wide.region_21.22_spmd.clone, body=%wide.region_16.21_spmd.clone.sunk | while | flops 506528256 | bytes 13381159 | solution.py:168
  50.2 2.1 %conditional.7 = (f32[128,6,128]{2,0,1:T(8,128)S(1)}, f32[512,256]{0,1:T(8,128)S(1)}) conditional(s32[]{:T(128)} %clamp.19, f32[128,6,128]{2,0,1:T(8,128)S(1)} %get-tuple-element.1421, (f32[128,6,128]{2,0,1:T(8,128)S(1)}, s32[]{:T(128)}, s32[]{:T(128)}, bf16[128,6,128]{0,2,1:T(8,128)(2,1)S(1)}, ...), branch_computations={%region_17.17_spmd, %region_18.18_spmd, %region_19.19_spmd, %regio... | conditional | flops 506528256 | bytes 10758676 | solution.py:61
  50.4 0.5 exponential_select_fusion.3
  51.2 0.4 multiply_convert_fusion
  52.5 0.8 constant_dynamic-update-slice_fusion.2
  53.4 2.1 %conditional.7 = (f32[128,6,128]{2,0,1:T(8,128)S(1)}, f32[512,256]{0,1:T(8,128)S(1)}) conditional(s32[]{:T(128)} %clamp.19, f32[128,6,128]{2,0,1:T(8,128)S(1)} %get-tuple-element.1421, (f32[128,6,128]{2,0,1:T(8,128)S(1)}, s32[]{:T(128)}, s32[]{:T(128)}, bf16[128,6,128]{0,2,1:T(8,128)(2,1)S(1)}, ...), branch_computations={%region_17.17_spmd, %region_18.18_spmd, %region_19.19_spmd, %regio... | conditional | flops 506528256 | bytes 10758676 | solution.py:61
  53.5 0.5 exponential_select_fusion.3
  55.7 0.9 constant_dynamic-update-slice_fusion.2
  56.9 0.9 constant_dynamic-update-slice_fusion.2
  58.1 0.9 constant_dynamic-update-slice_fusion.2
  58.9 2.9 %copy.78 = f32[16,128,256]{1,2,0:T(8,128)} copy(f32[16,128,256]{2,1,0:T(8,128)} %bitcast.88) | data formatting | bytes 4194304 | tf_op jit(solution)/shard_map/reshape | solution.py:176
  61.8 13.2 %all-to-all-start = ((f32[16,128,256]{1,2,0:T(8,128)}), f32[16,128,256]{1,2,0:T(8,128)S(1)}, u32[]{:S(2)}, u32[]{:S(2)}) async-start(f32[16,128,256]{1,2,0:T(8,128)} %copy.78), calls=%async_computation | async-start | bytes 4194304 | tf_op jit(solution)/shard_map/all_to_all | solution.py:175
  75.2 0.9 copy.80
  76.1 46.3 %all-to-all-done = f32[16,128,256]{1,2,0:T(8,128)S(1)} async-done(((f32[16,128,256]{1,2,0:T(8,128)}), f32[16,128,256]{1,2,0:T(8,128)S(1)}, u32[]{:S(2)}, u32[]{:S(2)}) %all-to-all-start) | async-done | bytes 2097184 | tf_op jit(solution)/shard_map/all_to_all | solution.py:175
  122.5 0.7 copy.82
  123.2 0.7 copy.81
  (76 shorter events, 5.1 us)
Async XLA Ops:
  0.6 4.1 %copy-start.1 = (bf16[128,128]{1,0:T(8,128)(2,1)S(1)}, bf16[128,128]{1,0:T(8,128)(2,1)}, u32[]{:S(2)}) copy-start(bf16[128,128]{1,0:T(8,128)(2,1)} %param.52) | copy-start | bytes 98308
  0.6 21.2 %copy-start.2 = (bf16[128,128]{1,0:T(8,128)(2,1)S(1)}, bf16[128,128]{1,0:T(8,128)(2,1)}, u32[]{:S(2)}) copy-start(bf16[128,128]{1,0:T(8,128)(2,1)} %param.53) | copy-start | bytes 98308
  58.9 2.9 %copy-start = (f32[128,6]{0,1:T(8,128)}, f32[128,6]{0,1:T(8,128)S(1)}, u32[]{:S(2)}) copy-start(f32[128,6]{0,1:T(8,128)S(1)} %get-tuple-element.1469) | copy-start | bytes 9220
  61.8 60.6 %all-to-all-start = ((f32[16,128,256]{1,2,0:T(8,128)}), f32[16,128,256]{1,2,0:T(8,128)S(1)}, u32[]{:S(2)}, u32[]{:S(2)}) async-start(f32[16,128,256]{1,2,0:T(8,128)} %copy.78), calls=%async_computation | async-start | bytes 4194304 | tf_op jit(solution)/shard_map/all_to_all | solution.py:175
where the time goes:
time: 124 us
  waiting for transfers between devices  46.3 us (37%)
  blocking collectives  39.9 us (32%)
  starting transfers between devices  13.2 us (11%)
  local copies, waits for them, and re-layouts  13.1 us (11%)
  matrix products  5.79 us (5%)
  other arithmetic  4.14 us (3%)
    all_to_all x1, waiting for transfers between devices, body(): lax.all_to_all(partial_sums.reshape(ctx_count, tok_rows, 2 * head_dim), '...  46.3 us
    all_gather x1, blocking collectives, body(): value_piece = lax.all_gather(value_rows, 'ctx', axis=0, tiled=True)  22.8 us
    all_gather x1, blocking collectives, body(): key_piece = lax.all_gather(key_rows, 'ctx', axis=0, tiled=True)  17.1 us
    all_to_all x1, starting transfers between devices, body(): lax.all_to_all(partial_sums.reshape(ctx_count, tok_rows, 2 * head_dim), '...  13.2 us
    dynamic_update_slice x8, local copies, waits for them, and re-layouts, backward_step(): lax.dynamic_update_slice_in_dim(partial_sums, block_sums, key_start, 0)  4.17 us
    unnamed x12, local copies, waits for them, and re-layouts  3.83 us
    reshape x1, local copies, waits for them, and re-layouts, body(): partial_sums.reshape(ctx_count, tok_rows, 2 * head_dim)  2.89 us
  transfers between devices with their start and end apart: 1, of which 1 were waited for; matrix products, arithmetic and copies ran while one was open for 1% of the time, Pallas kernels for 0%

commit v1 on v0

--- a/solution.py
+++ b/solution.py
@@ -94,7 +94,12 @@
     row_total = jnp.zeros((tok_rows, head_count), jnp.float32)
     weighted = jnp.zeros((tok_rows, head_count), jnp.float32)
     key_piece = lax.all_gather(key_rows, "ctx", axis=0, tiled=True)
-    value_piece = lax.all_gather(value_rows, "ctx", axis=0, tiled=True)
+    ring = [value_rows]
+    for hop in range(15):
+        ring.append(lax.ppermute(ring[-1], "ctx", [(dev, (dev + 1) % 16) for dev in range(16)]))
+    value_piece = jnp.roll(
+        jnp.concatenate(ring[::-1], axis=0), (lax.axis_index("ctx") + 1) * ring[0].shape[0], axis=0
+    )
     piece_rows = key_piece.shape[0]
     block_rows = math.gcd(piece_rows, 512)
 

time: 124 us -> 181 us (1.46)
  starting transfers between devices: 13.2 us -> 66.6 us
  waiting for transfers between devices: 46.3 us -> 57.9 us
  blocking collectives: 39.9 us -> 31.3 us
    ppermute x0 -> x15, starting transfers between devices: none -> 43.3 us  [body(): lax.ppermute(ring[-1], 'ctx', [(dev, (dev + 1) % 16) for dev in range(16)])]
    all_gather x1 -> x0, blocking collectives: 22.8 us -> none  [body(): value_piece = lax.all_gather(value_rows, 'ctx', axis=0, tiled=True)]
    all_gather x1, blocking collectives: 17.1 us -> 31.3 us  [body(): key_piece = lax.all_gather(key_rows, 'ctx', axis=0, tiled=True)]
    ppermute x0 -> x15, waiting for transfers between devices: none -> 11.6 us  [body(): lax.ppermute(ring[-1], 'ctx', [(dev, (dev + 1) % 16) for dev in range(16)])]
    all_to_all x1, starting transfers between devices: 13.2 us -> 23.3 us  [body(): lax.all_to_all(partial_sums.reshape(ctx_count, tok_rows, 2 * head_dim), '...]
    unnamed x12 -> x43, local copies, waits for them, and re-layouts: 3.83 us -> 3.2 us
  transfers between devices with their start and end apart: 1 -> 16, of which waited for: 1 -> 14; matrix products, arithmetic and copies ran while one was open for 1% -> 2% of each run, Pallas kernels for 0% -> 0%
where the time goes in v1:
time: 181 us; the launch traced here: 180 us
  starting transfers between devices  66.6 us (37%)
  waiting for transfers between devices  57.9 us (32%)
  blocking collectives  31.3 us (17%)
  local copies, waits for them, and re-layouts  12.5 us (7%)
  matrix products  5.79 us (3%)
  other arithmetic  4.13 us (2%)
    all_to_all x1, waiting for transfers between devices, body(): lax.all_to_all(partial_sums.reshape(ctx_count, tok_rows, 2 * head_dim), '...  46.3 us
    ppermute x15, starting transfers between devices, body(): lax.ppermute(ring[-1], 'ctx', [(dev, (dev + 1) % 16) for dev in range(16)])  43.3 us
    all_gather x1, blocking collectives, body(): key_piece = lax.all_gather(key_rows, 'ctx', axis=0, tiled=True)  31.3 us
    all_to_all x1, starting transfers between devices, body(): lax.all_to_all(partial_sums.reshape(ctx_count, tok_rows, 2 * head_dim), '...  23.3 us
    ppermute x15, waiting for transfers between devices, body(): lax.ppermute(ring[-1], 'ctx', [(dev, (dev + 1) % 16) for dev in range(16)])  11.6 us
    dynamic_update_slice x8, local copies, waits for them, and re-layouts, backward_step(): lax.dynamic_update_slice_in_dim(partial_sums, block_sums, key_start, 0)  4.13 us
  transfers between devices with their start and end apart: 16, of which 14 were waited for; matrix products, arithmetic and copies ran while one was open for 2% of the time, Pallas kernels for 0%

profile of v1, /device:TPU:13, one launch (start us, length us, event | category | flops | bytes accessed | tf_op | source)
XLA Modules:
  0.0 180.1 jit_solution(12439934738861543800)
XLA Ops:
  0.6 1.9 %collective-permute-start = (bf16[128,128]{1,0:T(8,128)(2,1)}, bf16[128,128]{1,0:T(8,128)(2,1)S(1)}, u32[]{:S(2)}, u32[]{:S(2)}) collective-permute-start(bf16[128,128]{1,0:T(8,128)(2,1)} %param.53), channel_id=1, source_target_pairs={{0,2},{2,4},{4,6},{6,8},{8,10},{10,12},{12,14},{14,16},{16,18},{18... | collective-permute-start | bytes 98312 | tf_op jit(solution)/shard_map/ppermute | solution.py:99
  2.5 1.3 collective-permute-done
  3.8 3.1 %collective-permute-start.1 = (bf16[128,128]{1,0:T(8,128)(2,1)S(1)}, bf16[128,128]{1,0:T(8,128)(2,1)S(1)}, u32[]{:S(2)}, u32[]{:S(2)}) collective-permute-start(bf16[128,128]{1,0:T(8,128)(2,1)S(1)} %collective-permute-done), channel_id=1, source_target_pairs={{0,2},{2,4},{4,6},{6,8},{8,10},{10,12},{12,14},{14,16},{16,18},{18... | collective-permute-start | bytes 98312 | tf_op jit(solution)/shard_map/ppermute | solution.py:99
  6.9 1.0 collective-permute-done.1
  8.0 3.2 %collective-permute-start.2 = (bf16[128,128]{1,0:T(8,128)(2,1)S(1)}, bf16[128,128]{1,0:T(8,128)(2,1)S(1)}, u32[]{:S(2)}, u32[]{:S(2)}) collective-permute-start(bf16[128,128]{1,0:T(8,128)(2,1)S(1)} %collective-permute-done.1), channel_id=1, source_target_pairs={{0,2},{2,4},{4,6},{6,8},{8,10},{10,12},{12,14},{14,16},{16,18},{18... | collective-permute-start | bytes 98312 | tf_op jit(solution)/shard_map/ppermute | solution.py:99
  11.2 1.0 collective-permute-done.2
  12.2 3.2 %collective-permute-start.3 = (bf16[128,128]{1,0:T(8,128)(2,1)S(1)}, bf16[128,128]{1,0:T(8,128)(2,1)S(1)}, u32[]{:S(2)}, u32[]{:S(2)}) collective-permute-start(bf16[128,128]{1,0:T(8,128)(2,1)S(1)} %collective-permute-done.2), channel_id=1, source_target_pairs={{0,2},{2,4},{4,6},{6,8},{8,10},{10,12},{12,14},{14,16},{16,18},{18... | collective-permute-start | bytes 98312 | tf_op jit(solution)/shard_map/ppermute | solution.py:99
  15.4 1.0 collective-permute-done.3
  16.4 3.2 %collective-permute-start.4 = (bf16[128,128]{1,0:T(8,128)(2,1)S(1)}, bf16[128,128]{1,0:T(8,128)(2,1)S(1)}, u32[]{:S(2)}, u32[]{:S(2)}) collective-permute-start(bf16[128,128]{1,0:T(8,128)(2,1)S(1)} %collective-permute-done.3), channel_id=1, source_target_pairs={{0,2},{2,4},{4,6},{6,8},{8,10},{10,12},{12,14},{14,16},{16,18},{18... | collective-permute-start | bytes 98312 | tf_op jit(solution)/shard_map/ppermute | solution.py:99
  19.7 1.0 collective-permute-done.4
  20.7 3.2 %collective-permute-start.5 = (bf16[128,128]{1,0:T(8,128)(2,1)S(1)}, bf16[128,128]{1,0:T(8,128)(2,1)S(1)}, u32[]{:S(2)}, u32[]{:S(2)}) collective-permute-start(bf16[128,128]{1,0:T(8,128)(2,1)S(1)} %collective-permute-done.4), channel_id=1, source_target_pairs={{0,2},{2,4},{4,6},{6,8},{8,10},{10,12},{12,14},{14,16},{16,18},{18... | collective-permute-start | bytes 98312 | tf_op jit(solution)/shard_map/ppermute | solution.py:99
  23.9 1.0 collective-permute-done.5
  24.9 3.2 %collective-permute-start.6 = (bf16[128,128]{1,0:T(8,128)(2,1)S(1)}, bf16[128,128]{1,0:T(8,128)(2,1)S(1)}, u32[]{:S(2)}, u32[]{:S(2)}) collective-permute-start(bf16[128,128]{1,0:T(8,128)(2,1)S(1)} %collective-permute-done.5), channel_id=1, source_target_pairs={{0,2},{2,4},{4,6},{6,8},{8,10},{10,12},{12,14},{14,16},{16,18},{18... | collective-permute-start | bytes 98312 | tf_op jit(solution)/shard_map/ppermute | solution.py:99
  28.1 1.0 collective-permute-done.6
  29.2 3.2 %collective-permute-start.7 = (bf16[128,128]{1,0:T(8,128)(2,1)S(1)}, bf16[128,128]{1,0:T(8,128)(2,1)S(1)}, u32[]{:S(2)}, u32[]{:S(2)}) collective-permute-start(bf16[128,128]{1,0:T(8,128)(2,1)S(1)} %collective-permute-done.6), channel_id=1, source_target_pairs={{0,2},{2,4},{4,6},{6,8},{8,10},{10,12},{12,14},{14,16},{16,18},{18... | collective-permute-start | bytes 98312 | tf_op jit(solution)/shard_map/ppermute | solution.py:99
  33.4 3.2 %collective-permute-start.8 = (bf16[128,128]{1,0:T(8,128)(2,1)S(1)}, bf16[128,128]{1,0:T(8,128)(2,1)S(1)}, u32[]{:S(2)}, u32[]{:S(2)}) collective-permute-start(bf16[128,128]{1,0:T(8,128)(2,1)S(1)} %collective-permute-done.7), channel_id=1, source_target_pairs={{0,2},{2,4},{4,6},{6,8},{8,10},{10,12},{12,14},{14,16},{16,18},{18... | collective-permute-start | bytes 98312 | tf_op jit(solution)/shard_map/ppermute | solution.py:99
  37.6 3.2 %collective-permute-start.9 = (bf16[128,128]{1,0:T(8,128)(2,1)S(1)}, bf16[128,128]{1,0:T(8,128)(2,1)S(1)}, u32[]{:S(2)}, u32[]{:S(2)}) collective-permute-start(bf16[128,128]{1,0:T(8,128)(2,1)S(1)} %collective-permute-done.8), channel_id=1, source_target_pairs={{0,2},{2,4},{4,6},{6,8},{8,10},{10,12},{12,14},{14,16},{16,18},{18... | collective-permute-start | bytes 98312 | tf_op jit(solution)/shard_map/ppermute | solution.py:99
  40.9 31.3 %all_gather.3 = bf16[2048,128]{1,0:T(8,128)(2,1)S(1)} all-gather(bf16[128,128]{1,0:T(8,128)(2,1)} %param.52), channel_id=1, replica_groups=mesh['ctx'=16,'head'=2] {'ctx'}, dimensions={0}, use_global_device_ids=true | all-gather | bytes 557056 | tf_op jit(solution)/shard_map/all_gather | solution.py:96
  73.4 3.0 %collective-permute-start.11 = (bf16[128,128]{1,0:T(8,128)(2,1)S(1)}, bf16[128,128]{1,0:T(8,128)(2,1)S(1)}, u32[]{:S(2)}, u32[]{:S(2)}) collective-permute-start(bf16[128,128]{1,0:T(8,128)(2,1)S(1)} %collective-permute-done.10), channel_id=1, source_target_pairs={{0,2},{2,4},{4,6},{6,8},{8,10},{10,12},{12,14},{14,16},{16,18},{18... | collective-permute-start | bytes 98312 | tf_op jit(solution)/shard_map/ppermute | solution.py:99
  77.5 3.2 %collective-permute-start.12 = (bf16[128,128]{1,0:T(8,128)(2,1)S(1)}, bf16[128,128]{1,0:T(8,128)(2,1)S(1)}, u32[]{:S(2)}, u32[]{:S(2)}) collective-permute-start(bf16[128,128]{1,0:T(8,128)(2,1)S(1)} %collective-permute-done.11), channel_id=1, source_target_pairs={{0,2},{2,4},{4,6},{6,8},{8,10},{10,12},{12,14},{14,16},{16,18},{18... | collective-permute-start | bytes 98312 | tf_op jit(solution)/shard_map/ppermute | solution.py:99
  81.7 3.2 %collective-permute-start.13 = (bf16[128,128]{1,0:T(8,128)(2,1)S(1)}, bf16[128,128]{1,0:T(8,128)(2,1)S(1)}, u32[]{:S(2)}, u32[]{:S(2)}) collective-permute-start(bf16[128,128]{1,0:T(8,128)(2,1)S(1)} %collective-permute-done.12), channel_id=1, source_target_pairs={{0,2},{2,4},{4,6},{6,8},{8,10},{10,12},{12,14},{14,16},{16,18},{18... | collective-permute-start | bytes 98312 | tf_op jit(solution)/shard_map/ppermute | solution.py:99
  86.0 3.2 %collective-permute-start.14 = (bf16[128,128]{1,0:T(8,128)(2,1)S(1)}, bf16[128,128]{1,0:T(8,128)(2,1)S(1)}, u32[]{:S(2)}, u32[]{:S(2)}) collective-permute-start(bf16[128,128]{1,0:T(8,128)(2,1)S(1)} %collective-permute-done.13), channel_id=1, source_target_pairs={{0,2},{2,4},{4,6},{6,8},{8,10},{10,12},{12,14},{14,16},{16,18},{18... | collective-permute-start | bytes 98312 | tf_op jit(solution)/shard_map/ppermute | solution.py:99
  90.8 3.9 %while.53 = (s32[]{:T(128)}, f32[128,6]{0,1:T(8,128)S(1)}, f32[128,6]{0,1:T(8,128)S(1)}, f32[128,6]{0,1:T(8,128)S(1)}, s32[]{:T(128)}, /*index=5*/s32[]{:T(128)}...) while((s32[]{:T(128)}, f32[128,6]{0,1:T(8,128)S(1)}, ...), condition=%wide.region_15.16_spmd.clone, body=%wide.region_1.15_spmd.clone.sunk | while | flops 205327120 | bytes 6221379 | solution.py:112
  90.8 1.7 conditional.6
  92.7 1.7 conditional.6
  94.7 1.5 broadcast_in_dim.124.clone
  96.2 8.7 %while.54 = (s32[]{:T(128)}, f32[128,6,128]{2,0,1:T(8,128)S(1)}, f32[2048,256]{1,0:T(8,128)}, s32[]{:T(128)}, s32[]{:T(128)}, /*index=5*/bf16[2048,128]{1,0:T(8,...) while((s32[]{:T(128)}, f32[128,6,128]{2,0,1:T(8,128)S(1)}, ...), condition=%wide.region_21.22_spmd.clone, body=%wide.region_16.21_spmd.clone.sunk | while | flops 506528256 | bytes 13381159 | solution.py:173
  96.2 2.1 %conditional.7 = (f32[128,6,128]{2,0,1:T(8,128)S(1)}, f32[512,256]{0,1:T(8,128)S(1)}) conditional(s32[]{:T(128)} %clamp.19, f32[128,6,128]{2,0,1:T(8,128)S(1)} %get-tuple-element.1421, (f32[128,6,128]{2,0,1:T(8,128)S(1)}, s32[]{:T(128)}, s32[]{:T(128)}, bf16[128,6,128]{0,2,1:T(8,128)(2,1)S(1)}, ...), branch_computations={%region_17.17_spmd, %region_18.18_spmd, %region_19.19_spmd, %regio... | conditional | flops 506528256 | bytes 10758676 | solution.py:61
  99.4 2.1 %conditional.7 = (f32[128,6,128]{2,0,1:T(8,128)S(1)}, f32[512,256]{0,1:T(8,128)S(1)}) conditional(s32[]{:T(128)} %clamp.19, f32[128,6,128]{2,0,1:T(8,128)S(1)} %get-tuple-element.1421, (f32[128,6,128]{2,0,1:T(8,128)S(1)}, s32[]{:T(128)}, s32[]{:T(128)}, bf16[128,6,128]{0,2,1:T(8,128)(2,1)S(1)}, ...), branch_computations={%region_17.17_spmd, %region_18.18_spmd, %region_19.19_spmd, %regio... | conditional | flops 506528256 | bytes 10758676 | solution.py:61
  104.9 2.9 %copy.78 = f32[16,128,256]{1,2,0:T(8,128)} copy(f32[16,128,256]{2,1,0:T(8,128)} %bitcast.88) | data formatting | bytes 4194304 | tf_op jit(solution)/shard_map/reshape | solution.py:181
  107.8 23.3 %all-to-all-start = ((f32[16,128,256]{1,2,0:T(8,128)}), f32[16,128,256]{1,2,0:T(8,128)S(1)}, u32[]{:S(2)}, u32[]{:S(2)}) async-start(f32[16,128,256]{1,2,0:T(8,128)} %copy.78), calls=%async_computation | async-start | bytes 4194304 | tf_op jit(solution)/shard_map/all_to_all | solution.py:180
  132.2 46.3 %all-to-all-done = f32[16,128,256]{1,2,0:T(8,128)S(1)} async-done(((f32[16,128,256]{1,2,0:T(8,128)}), f32[16,128,256]{1,2,0:T(8,128)S(1)}, u32[]{:S(2)}, u32[]{:S(2)}) %all-to-all-start) | async-done | bytes 2097184 | tf_op jit(solution)/shard_map/all_to_all | solution.py:180
  (138 shorter events, 22.4 us)
Async XLA Ops:
  0.6 89.0 %copy-start = (bf16[128,768]{1,0:T(8,128)(2,1)S(1)}, bf16[128,768]{1,0:T(8,128)(2,1)}, u32[]{:S(2)}) copy-start(bf16[128,768]{1,0:T(8,128)(2,1)} %param.51) | copy-start | bytes 589828
  0.6 3.2 %collective-permute-start = (bf16[128,128]{1,0:T(8,128)(2,1)}, bf16[128,128]{1,0:T(8,128)(2,1)S(1)}, u32[]{:S(2)}, u32[]{:S(2)}) collective-permute-start(bf16[128,128]{1,0:T(8,128)(2,1)} %param.53), channel_id=1, source_target_pairs={{0,2},{2,4},{4,6},{6,8},{8,10},{10,12},{12,14},{14,16},{16,18},{18... | collective-permute-start | bytes 98312 | tf_op jit(solution)/shard_map/ppermute | solution.py:99
  3.8 4.1 %collective-permute-start.1 = (bf16[128,128]{1,0:T(8,128)(2,1)S(1)}, bf16[128,128]{1,0:T(8,128)(2,1)S(1)}, u32[]{:S(2)}, u32[]{:S(2)}) collective-permute-start(bf16[128,128]{1,0:T(8,128)(2,1)S(1)} %collective-permute-done), channel_id=1, source_target_pairs={{0,2},{2,4},{4,6},{6,8},{8,10},{10,12},{12,14},{14,16},{16,18},{18... | collective-permute-start | bytes 98312 | tf_op jit(solution)/shard_map/ppermute | solution.py:99
  8.0 4.2 %collective-permute-start.2 = (bf16[128,128]{1,0:T(8,128)(2,1)S(1)}, bf16[128,128]{1,0:T(8,128)(2,1)S(1)}, u32[]{:S(2)}, u32[]{:S(2)}) collective-permute-start(bf16[128,128]{1,0:T(8,128)(2,1)S(1)} %collective-permute-done.1), channel_id=1, source_target_pairs={{0,2},{2,4},{4,6},{6,8},{8,10},{10,12},{12,14},{14,16},{16,18},{18... | collective-permute-start | bytes 98312 | tf_op jit(solution)/shard_map/ppermute | solution.py:99
  12.2 4.2 %collective-permute-start.3 = (bf16[128,128]{1,0:T(8,128)(2,1)S(1)}, bf16[128,128]{1,0:T(8,128)(2,1)S(1)}, u32[]{:S(2)}, u32[]{:S(2)}) collective-permute-start(bf16[128,128]{1,0:T(8,128)(2,1)S(1)} %collective-permute-done.2), channel_id=1, source_target_pairs={{0,2},{2,4},{4,6},{6,8},{8,10},{10,12},{12,14},{14,16},{16,18},{18... | collective-permute-start | bytes 98312 | tf_op jit(solution)/shard_map/ppermute | solution.py:99
  16.4 4.2 %collective-permute-start.4 = (bf16[128,128]{1,0:T(8,128)(2,1)S(1)}, bf16[128,128]{1,0:T(8,128)(2,1)S(1)}, u32[]{:S(2)}, u32[]{:S(2)}) collective-permute-start(bf16[128,128]{1,0:T(8,128)(2,1)S(1)} %collective-permute-done.3), channel_id=1, source_target_pairs={{0,2},{2,4},{4,6},{6,8},{8,10},{10,12},{12,14},{14,16},{16,18},{18... | collective-permute-start | bytes 98312 | tf_op jit(solution)/shard_map/ppermute | solution.py:99
  20.7 4.2 %collective-permute-start.5 = (bf16[128,128]{1,0:T(8,128)(2,1)S(1)}, bf16[128,128]{1,0:T(8,128)(2,1)S(1)}, u32[]{:S(2)}, u32[]{:S(2)}) collective-permute-start(bf16[128,128]{1,0:T(8,128)(2,1)S(1)} %collective-permute-done.4), channel_id=1, source_target_pairs={{0,2},{2,4},{4,6},{6,8},{8,10},{10,12},{12,14},{14,16},{16,18},{18... | collective-permute-start | bytes 98312 | tf_op jit(solution)/shard_map/ppermute | solution.py:99
  24.9 4.2 %collective-permute-start.6 = (bf16[128,128]{1,0:T(8,128)(2,1)S(1)}, bf16[128,128]{1,0:T(8,128)(2,1)S(1)}, u32[]{:S(2)}, u32[]{:S(2)}) collective-permute-start(bf16[128,128]{1,0:T(8,128)(2,1)S(1)} %collective-permute-done.5), channel_id=1, source_target_pairs={{0,2},{2,4},{4,6},{6,8},{8,10},{10,12},{12,14},{14,16},{16,18},{18... | collective-permute-start | bytes 98312 | tf_op jit(solution)/shard_map/ppermute | solution.py:99
  29.2 4.2 %collective-permute-start.7 = (bf16[128,128]{1,0:T(8,128)(2,1)S(1)}, bf16[128,128]{1,0:T(8,128)(2,1)S(1)}, u32[]{:S(2)}, u32[]{:S(2)}) collective-permute-start(bf16[128,128]{1,0:T(8,128)(2,1)S(1)} %collective-permute-done.6), channel_id=1, source_target_pairs={{0,2},{2,4},{4,6},{6,8},{8,10},{10,12},{12,14},{14,16},{16,18},{18... | collective-permute-start | bytes 98312 | tf_op jit(solution)/shard_map/ppermute | solution.py:99
  33.4 4.2 %collective-permute-start.8 = (bf16[128,128]{1,0:T(8,128)(2,1)S(1)}, bf16[128,128]{1,0:T(8,128)(2,1)S(1)}, u32[]{:S(2)}, u32[]{:S(2)}) collective-permute-start(bf16[128,128]{1,0:T(8,128)(2,1)S(1)} %collective-permute-done.7), channel_id=1, source_target_pairs={{0,2},{2,4},{4,6},{6,8},{8,10},{10,12},{12,14},{14,16},{16,18},{18... | collective-permute-start | bytes 98312 | tf_op jit(solution)/shard_map/ppermute | solution.py:99
  37.6 34.6 %collective-permute-start.9 = (bf16[128,128]{1,0:T(8,128)(2,1)S(1)}, bf16[128,128]{1,0:T(8,128)(2,1)S(1)}, u32[]{:S(2)}, u32[]{:S(2)}) collective-permute-start(bf16[128,128]{1,0:T(8,128)(2,1)S(1)} %collective-permute-done.8), channel_id=1, source_target_pairs={{0,2},{2,4},{4,6},{6,8},{8,10},{10,12},{12,14},{14,16},{16,18},{18... | collective-permute-start | bytes 98312 | tf_op jit(solution)/shard_map/ppermute | solution.py:99
  72.2 18.2 %copy-start.2 = (bf16[128,128]{1,0:T(8,128)(2,1)S(1)}, bf16[128,128]{1,0:T(8,128)(2,1)}, u32[]{:S(2)}) copy-start(bf16[128,128]{1,0:T(8,128)(2,1)} %param.53) | copy-start | bytes 98308
  72.2 1.2 collective-permute-start.10
  73.4 4.1 %collective-permute-start.11 = (bf16[128,128]{1,0:T(8,128)(2,1)S(1)}, bf16[128,128]{1,0:T(8,128)(2,1)S(1)}, u32[]{:S(2)}, u32[]{:S(2)}) collective-permute-start(bf16[128,128]{1,0:T(8,128)(2,1)S(1)} %collective-permute-done.10), channel_id=1, source_target_pairs={{0,2},{2,4},{4,6},{6,8},{8,10},{10,12},{12,14},{14,16},{16,18},{18... | collective-permute-start | bytes 98312 | tf_op jit(solution)/shard_map/ppermute | solution.py:99
  77.5 4.3 %collective-permute-start.12 = (bf16[128,128]{1,0:T(8,128)(2,1)S(1)}, bf16[128,128]{1,0:T(8,128)(2,1)S(1)}, u32[]{:S(2)}, u32[]{:S(2)}) collective-permute-start(bf16[128,128]{1,0:T(8,128)(2,1)S(1)} %collective-permute-done.11), channel_id=1, source_target_pairs={{0,2},{2,4},{4,6},{6,8},{8,10},{10,12},{12,14},{14,16},{16,18},{18... | collective-permute-start | bytes 98312 | tf_op jit(solution)/shard_map/ppermute | solution.py:99
  81.7 4.2 %collective-permute-start.13 = (bf16[128,128]{1,0:T(8,128)(2,1)S(1)}, bf16[128,128]{1,0:T(8,128)(2,1)S(1)}, u32[]{:S(2)}, u32[]{:S(2)}) collective-permute-start(bf16[128,128]{1,0:T(8,128)(2,1)S(1)} %collective-permute-done.12), channel_id=1, source_target_pairs={{0,2},{2,4},{4,6},{6,8},{8,10},{10,12},{12,14},{14,16},{16,18},{18... | collective-permute-start | bytes 98312 | tf_op jit(solution)/shard_map/ppermute | solution.py:99
  86.0 4.2 %collective-permute-start.14 = (bf16[128,128]{1,0:T(8,128)(2,1)S(1)}, bf16[128,128]{1,0:T(8,128)(2,1)S(1)}, u32[]{:S(2)}, u32[]{:S(2)}) collective-permute-start(bf16[128,128]{1,0:T(8,128)(2,1)S(1)} %collective-permute-done.13), channel_id=1, source_target_pairs={{0,2},{2,4},{4,6},{6,8},{8,10},{10,12},{12,14},{14,16},{16,18},{18... | collective-permute-start | bytes 98312 | tf_op jit(solution)/shard_map/ppermute | solution.py:99
  104.9 2.9 %copy-start.1 = (f32[128,6]{0,1:T(8,128)}, f32[128,6]{0,1:T(8,128)S(1)}, u32[]{:S(2)}) copy-start(f32[128,6]{0,1:T(8,128)S(1)} %get-tuple-element.1469) | copy-start | bytes 9220
  107.8 70.7 %all-to-all-start = ((f32[16,128,256]{1,2,0:T(8,128)}), f32[16,128,256]{1,2,0:T(8,128)S(1)}, u32[]{:S(2)}, u32[]{:S(2)}) async-start(f32[16,128,256]{1,2,0:T(8,128)} %copy.78), calls=%async_computation | async-start | bytes 4194304 | tf_op jit(solution)/shard_map/all_to_all | solution.py:180
